TPU v7x, 128 devices: a whole 4x4x4 slice. The times are simulated.
128 devices in a mesh: dp: 64 (over x, y_lo, z, core), mp: 2 (over y_hi).
Axes of the slice: x: 4, y: 4 (y_hi: 2, y_lo: 2; y = y_hi * 2 + y_lo), z: 4, core: 2. Of those that a mesh axis runs over, the one named last changes fastest.
Arguments:
- tokens: bfloat16 [65536, 1152], P('dp'), may hold values from -8 to 8
- lengths: int32 [1024], P('dp'), may hold values from 1 to 64, as said below
- images: bfloat16 [1024, 1152], P('dp'), may hold values from -12 to 12
- pair_group: int32 [1024], replicated, may hold values from 0 to 511, never falling along the last dimension, each value on 1 to 4 neighbouring positions
- w_up: bfloat16 [1152, 4304], P(None, 'mp'), may hold values from -0.1875 to 0.1875
- w_down: bfloat16 [1152, 4304], P(None, 'mp'), may hold values from -0.09375 to 0.09375
Outputs:
- caption_loss: float32 [1024], P('dp')
- image_grad: float32 [1024, 1152], P('dp')
- up_grad: float32 [1152, 4304], P('dp', 'mp')
- down_grad: float32 [1152, 4304], P('dp', 'mp')
Inputs may be any that keep to these rules, and one draw needn't show every extreme that they name: Positions below lengths[c] of caption c are real tokens, the rest padding. `pair_group`: ids never fall along the pairs, and each id is held by 1 to 4 consecutive pairs.
All inputs are finite; a program needn't handle non-finite values.
Results may differ from a plain program's by a relative error of at most 0.0033.
Values may be sent and summed in bfloat16 or wider, within the bound.
No kernel may reach another device: no remote copies, remote signals or barrier semaphores. Data moves between devices by JAX's collectives and lax.ppermute only.
A program may use at most 192 MiB of HBM per device.

v0:
```python
import jax
import jax.numpy as jnp
from jax import lax
from jax.sharding import PartitionSpec as P

LOGIT_SCALE = 117.0
LOGIT_SHIFT = -12.9


def passed_along(value, axis, steps):
    count = lax.axis_size(axis)
    pairs = [(source, (source + steps) % count) for source in range(count)]
    return lax.ppermute(value, axis, pairs)


def layer_norm(rows):
    center = rows - jnp.mean(rows, -1, keepdims=True)
    spread = jnp.mean(center * center, -1, keepdims=True)
    return center * lax.rsqrt(spread + 1e-06)


def gelu_pair(pre):
    const = 0.7978845608028654
    inner = const * (pre + 0.044715 * pre * pre * pre)
    tanh_u = jnp.tanh(inner)
    value = 0.5 * pre * (1.0 + tanh_u)
    slope = 0.5 * (1.0 + tanh_u) + 0.5 * pre * (1.0 - tanh_u * tanh_u) * const * (
        1.0 + 3.0 * 0.044715 * pre * pre
    )
    return (value, slope)


def unit_rows(rows):
    scale = lax.rsqrt(jnp.sum(rows * rows, 1, keepdims=True) + 1e-06)
    return (rows * scale, scale)


def pair_terms(text_rows, text_group, image_half, image_group, total):
    logits = (
        LOGIT_SCALE
        * lax.dot_general(
            text_rows, image_half, (((1,), (1,)), ((), ())), preferred_element_type=jnp.float32
        )
        + LOGIT_SHIFT
    )
    signs = jnp.where(text_group[:, None] == image_group[None, :], 1.0, -1.0).astype(jnp.float32)
    loss_terms = -jnp.sum(jax.nn.log_sigmoid(signs * logits), 1) / total
    coef = (-LOGIT_SCALE * signs * jax.nn.sigmoid(-signs * logits)).astype(jnp.bfloat16)
    grad_terms = jnp.dot(coef, image_half, preferred_element_type=jnp.float32)
    image_terms = lax.dot_general(
        coef, text_rows, (((0,), (0,)), ((), ())), preferred_element_type=jnp.float32
    )
    return (loss_terms, grad_terms, image_terms)


def on_device(tokens, lengths, images, pair_group, w_up, w_down):
    captions = lengths.shape[0]
    seq_len = tokens.shape[0] // captions
    width = tokens.shape[1]
    hidden = w_up.shape[1]
    devices = lax.axis_size("dp")
    own_index = lax.axis_index("dp")
    total = captions * devices
    tok_float = tokens.astype(jnp.float32)
    normed = layer_norm(tok_float).astype(jnp.bfloat16)
    pre = jnp.dot(normed, w_up, preferred_element_type=jnp.float32)
    value, slope = gelu_pair(pre)
    position = jnp.arange(seq_len, dtype=jnp.int32)
    valid = (position[None, :] < lengths[:, None]).astype(jnp.float32)
    share = valid / jnp.sum(valid, 1, keepdims=True)
    gmean = jnp.sum(value.reshape(captions, seq_len, hidden) * share[:, :, None], 1)
    tmean = jnp.sum(tok_float.reshape(captions, seq_len, width) * share[:, :, None], 1)
    gbar = gmean.astype(jnp.bfloat16)
    partial_value = lax.dot_general(
        gbar, w_down, (((1,), (1,)), ((), ())), preferred_element_type=jnp.float32
    )
    pooled = tmean + lax.psum(partial_value, "mp")
    unit_text, text_scale = unit_rows(pooled)
    unit_image, image_scale = unit_rows(images.astype(jnp.float32))
    text_half = unit_text.astype(jnp.bfloat16)
    image_half = unit_image.astype(jnp.bfloat16)
    image_group = lax.dynamic_slice_in_dim(pair_group, own_index * captions, captions)

    def visit(turn, text_rows, acc_grad, acc_loss, img_back):
        anchor = (own_index - turn) % devices
        text_group = lax.dynamic_slice_in_dim(pair_group, anchor * captions, captions)
        loss_terms, grad_terms, image_terms = pair_terms(
            text_rows, text_group, image_half, image_group, total
        )
        return (acc_grad + grad_terms, acc_loss + loss_terms, img_back + image_terms)

    def carry_home(acc_grad, acc_loss):
        return passed_along((acc_grad, acc_loss), "dp", 1)

    def cycle_step(turn, state):
        text_rows, acc_grad, acc_loss, img_back = state
        acc_grad, acc_loss, img_back = visit(turn, text_rows, acc_grad, acc_loss, img_back)
        text_rows = passed_along(text_rows, "dp", 1)
        acc_grad, acc_loss = carry_home(acc_grad, acc_loss)
        return (text_rows, acc_grad, acc_loss, img_back)

    start = (
        text_half,
        jnp.zeros((captions, width), jnp.float32),
        jnp.zeros((captions,), jnp.float32),
        jnp.zeros((captions, width), jnp.float32),
    )
    text_rows, acc_grad, acc_loss, img_back = lax.fori_loop(0, devices - 1, cycle_step, start)
    acc_grad, acc_loss, img_back = visit(devices - 1, text_rows, acc_grad, acc_loss, img_back)
    text_back, caption_loss = carry_home(acc_grad, acc_loss)
    pooled_grad = (
        text_back - unit_text * jnp.sum(unit_text * text_back, 1, keepdims=True)
    ) * text_scale
    image_grad = (
        img_back - unit_image * jnp.sum(unit_image * img_back, 1, keepdims=True)
    ) * image_scale
    pooled_half = pooled_grad.astype(jnp.bfloat16)
    hidden_grad = jnp.dot(pooled_half, w_down, preferred_element_type=jnp.float32)
    pre_grad = (
        share[:, :, None] * hidden_grad[:, None, :] * slope.reshape(captions, seq_len, hidden)
    ).astype(jnp.bfloat16)
    pre_grad = pre_grad.reshape(captions * seq_len, hidden)
    down_term = lax.dot_general(
        pooled_half, gbar, (((0,), (0,)), ((), ())), preferred_element_type=jnp.float32
    )
    both = lax.psum_scatter(
        jnp.concatenate(
            [
                lax.dot_general(
                    normed, pre_grad, (((0,), (0,)), ((), ())), preferred_element_type=jnp.float32
                ),
                down_term,
            ],
            1,
        ),
        "dp",
        scatter_dimension=0,
        tiled=True,
    )
    up_grad = both[:, :hidden]
    down_grad = both[:, hidden:]
    return (caption_loss, image_grad, up_grad, down_grad)


def solution(mesh):
    in_specs = (P("dp", None), P("dp"), P("dp", None), P(), P(None, "mp"), P(None, "mp"))
    out_specs = (P("dp"), P("dp", None), P("dp", "mp"), P("dp", "mp"))
    return jax.shard_map(
        on_device, mesh=mesh, in_specs=in_specs, out_specs=out_specs, check_vma=False
    )
```

profile of v0, /device:TPU:0, one launch (start us, length us, event | category | flops | bytes accessed | tf_op | source)
XLA Modules:
  0.0 1348.7 jit_solution(15541220683048195390)
XLA Ops:
  13.3 14.8 %add_multiply_fusion = (f32[1024,2152]{0,1:T(8,128)}, f32[1024,2152]{0,1:T(8,128)}) fusion(bf16[1152,2152]{0,1:T(8,128)(2,1)} %param.12, bf16[1024,1152]{1,0:T(8,128)(2,1)} %param.8, f32[1024]{0:T(1024)S(1)} %add_rsqrt_fusion, f32[1024]{0:T(1024)S(1)} %broadcast_multiply_fusion), kind=kOutput, calls=%fused_computation.29 | convolution fusion | flops 5099552768 | bytes 24954880 | tf_op jit(solution)/shard_map/dot_general | solution.py:66
  28.0 9.2 copy.17
  48.0 29.6 %all-reduce.4.cloned.1.call-done = f32[16,1152]{1,0:T(8,128)} async-done(((f32[16,1152]{1,0:T(8,128)}), f32[16,1152]{1,0:T(8,128)}) %all-reduce.4.cloned.1.call-update) | async-done | bytes 73744 | tf_op jit(solution)/shard_map/psum | solution.py:77
  78.7 598.2 %while.22 = (s32[]{:T(128)}, bf16[16,1152]{1,0:T(8,128)(2,1)S(1)}, f32[16,1152]{1,0:T(8,128)S(1)}, f32[16]{0:T(128)S(1)}, f32[16,1152]{1,0:T(8,128)S(1)}, /*inde...) while((s32[]{:T(128)}, bf16[16,1152]{1,0:T(8,128)(2,1)S(1)}, ...), condition=%wide.region_10.11_spmd.clone, body=%wide.region_8.10_spmd.clone.sunk | while | flops 1833251 | bytes 963002 | solution.py:108
  90.7 7.7 collective-permute-done.2
  100.2 7.7 collective-permute-done.2
  109.7 7.7 collective-permute-done.2
  119.2 7.7 collective-permute-done.2
  128.7 7.7 collective-permute-done.2
  138.1 7.7 collective-permute-done.2
  147.6 7.7 collective-permute-done.2
  157.1 7.7 collective-permute-done.2
  166.6 7.7 collective-permute-done.2
  176.1 7.7 collective-permute-done.2
  185.6 7.7 collective-permute-done.2
  195.0 7.7 collective-permute-done.2
  204.5 7.7 collective-permute-done.2
  214.0 7.7 collective-permute-done.2
  223.5 7.7 collective-permute-done.2
  233.0 7.7 collective-permute-done.2
  261.4 7.7 collective-permute-done.2
  270.9 7.7 collective-permute-done.2
  280.4 7.7 collective-permute-done.2
  289.9 7.7 collective-permute-done.2
  299.4 7.7 collective-permute-done.2
  356.3 7.7 collective-permute-done.2
  365.7 7.7 collective-permute-done.2
  375.2 7.7 collective-permute-done.2
  384.7 7.7 collective-permute-done.2
  441.6 7.7 collective-permute-done.2
  451.1 7.7 collective-permute-done.2
  460.6 7.7 collective-permute-done.2
  470.1 7.7 collective-permute-done.2
  479.5 7.7 collective-permute-done.2
  536.4 7.7 collective-permute-done.2
  545.9 7.7 collective-permute-done.2
  555.4 7.7 collective-permute-done.2
  564.9 7.7 collective-permute-done.2
  621.8 7.7 collective-permute-done.2
  631.3 7.7 collective-permute-done.2
  640.8 7.7 collective-permute-done.2
  650.2 7.7 collective-permute-done.2
  659.7 7.7 collective-permute-done.2
  677.7 7.9 collective-permute-done.4
  696.9 9.6 copy.18
  706.5 17.1 %fusion.19 = f32[1152,2152]{0,1:T(8,128)} fusion(f32[1024,2152]{0,1:T(8,128)} %get-tuple-element.301, f32[1024,2152]{0,1:T(8,128)} %copy.18, f32[1024]{0:T(1024)S(1)} %div.49, bf16[1024,1152]{1,0:T(8,128)(2,1)} %param.8, f32[1024]{0:T(1024)S(1)} %add_rsqrt_fusion, f32[1024]{0:T(1024)S(1)} %broadcast_multiply_fusion), kind=kOutput, calls=%fused_computation.33 | convolution fusion | flops 5125996544 | bytes 29917184 | tf_op jit(solution)/shard_map/dot_general | solution.py:129
  723.6 11.5 pad_maximum_fusion
  744.3 592.0 %all-reduce.6.cloned.1.call-done = f32[1152,4304]{0,1:T(8,128)} async-done(((f32[1152,4304]{0,1:T(8,128)}), f32[1152,4304]{0,1:T(8,128)}) %all-reduce.6.cloned.1.call-update) | async-done | bytes 19832848
  (776 shorter events, 334.6 us)
Async XLA Ops:
  7.2 70.4 %all-reduce.4.cloned.1.call-start = ((), (), s32[]{:S(2)}) async-start(), calls=%async_computation | async-start | bytes 147456 | tf_op jit(solution)/shard_map/psum | solution.py:77
  46.0 1290.3 %all-reduce.6.cloned.1.call-start = ((), (), s32[]{:S(2)}) async-start(), calls=%async_computation.1 | async-start | bytes 39665664
  78.8 10.2 collective-permute-start
  89.0 9.5 collective-permute-start
  98.5 9.5 collective-permute-start
  108.0 9.5 collective-permute-start
  117.5 9.5 collective-permute-start
  126.9 9.5 collective-permute-start
  136.4 9.5 collective-permute-start
  145.9 9.5 collective-permute-start
  155.4 9.5 collective-permute-start
  164.9 9.5 collective-permute-start
  174.4 9.5 collective-permute-start
  183.8 9.5 collective-permute-start
  193.3 9.5 collective-permute-start
  202.8 9.5 collective-permute-start
  212.3 9.5 collective-permute-start
  221.8 9.5 collective-permute-start
  231.3 9.5 collective-permute-start
  240.7 9.5 collective-permute-start
  250.2 9.5 collective-permute-start
  259.7 9.5 collective-permute-start
  269.2 9.5 collective-permute-start
  278.7 9.5 collective-permute-start
  288.2 9.5 collective-permute-start
  297.6 9.5 collective-permute-start
  307.1 9.5 collective-permute-start
  316.6 9.5 collective-permute-start
  326.1 9.5 collective-permute-start
  335.6 9.5 collective-permute-start
  345.1 9.5 collective-permute-start
  354.5 9.5 collective-permute-start
  364.0 9.5 collective-permute-start
  373.5 9.5 collective-permute-start
  383.0 9.5 collective-permute-start
  392.5 9.5 collective-permute-start
  402.0 9.5 collective-permute-start
  411.4 9.5 collective-permute-start
  420.9 9.5 collective-permute-start
  430.4 9.5 collective-permute-start
  449.4 9.5 collective-permute-start
  458.9 9.5 collective-permute-start
  468.3 9.5 collective-permute-start
  544.2 9.5 collective-permute-start
  553.7 9.5 collective-permute-start
  629.5 9.5 collective-permute-start
  639.0 9.5 collective-permute-start
  648.5 9.5 collective-permute-start
  (153 other events, 1929.7 us)
Sparse Core Ops, SparseCore 0:
  46.1 31.4 all-reduce.3
  735.3 600.9 all-reduce.5
where the time goes:
time: 1350 us
  waiting for transfers between devices  1120 us (83%)
  matrix products  84.2 us (6%)
  local copies, waits for them, and re-layouts  79 us (6%)
  other arithmetic  25.9 us (2%)
  starting transfers between devices  16.2 us (1%)
  between operations  14.9 us (1%)
    unnamed x3, waiting for transfers between devices  592 us
    ppermute x191, waiting for transfers between devices, passed_along(): return lax.ppermute(value, axis, pairs)  502 us
    dynamic_slice x64, local copies, waits for them, and re-layouts, visit(): lax.dynamic_slice_in_dim(pair_group, anchor * captions, captions)  49 us
    psum x1, waiting for transfers between devices, on_device(): pooled = tmean + lax.psum(partial_value, 'mp')  29.6 us
  transfers between devices with their start and end apart: 193, of which 67 were waited for; matrix products, arithmetic and copies ran while one was open for 7% of the time, Pallas kernels for 0%

commit v1 on v0

v1 whole, which is shorter than its diff:
```python
import jax
import jax.numpy as jnp
from jax import lax
from jax.experimental.layout import Layout, with_layout_constraint
from jax.sharding import PartitionSpec as P

LOGIT_SCALE = 117.0
LOGIT_SHIFT = -12.9


def passed_along(value, axis, steps):
    count = lax.axis_size(axis)
    pairs = [(source, (source + steps) % count) for source in range(count)]
    return lax.ppermute(value, axis, pairs)


def layer_norm(rows):
    center = rows - jnp.mean(rows, -1, keepdims=True)
    spread = jnp.mean(center * center, -1, keepdims=True)
    return center * lax.rsqrt(spread + 1e-06)


def gelu_pair(pre):
    const = 0.7978845608028654
    inner = const * (pre + 0.044715 * pre * pre * pre)
    tanh_u = jnp.tanh(inner)
    value = 0.5 * pre * (1.0 + tanh_u)
    slope = 0.5 * (1.0 + tanh_u) + 0.5 * pre * (1.0 - tanh_u * tanh_u) * const * (
        1.0 + 3.0 * 0.044715 * pre * pre
    )
    return (value, slope)


def unit_rows(rows):
    scale = lax.rsqrt(jnp.sum(rows * rows, 1, keepdims=True) + 1e-06)
    return (rows * scale, scale)


def pair_coef(own_rows, own_group, other_rows, other_group):
    logits = (
        LOGIT_SCALE
        * lax.dot_general(
            own_rows, other_rows, (((1,), (1,)), ((), ())), preferred_element_type=jnp.float32
        )
        + LOGIT_SHIFT
    )
    signs = jnp.where(own_group[:, None] == other_group[None, :], 1.0, -1.0).astype(jnp.float32)
    coef = (-LOGIT_SCALE * signs * jax.nn.sigmoid(-signs * logits)).astype(jnp.bfloat16)
    return (logits, signs, coef)


def on_device(tokens, lengths, images, pair_group, w_up, w_down):
    captions = lengths.shape[0]
    seq_len = tokens.shape[0] // captions
    width = tokens.shape[1]
    hidden = w_up.shape[1]
    devices = lax.axis_size("dp")
    own_index = lax.axis_index("dp")
    total = captions * devices
    own_group = lax.dynamic_slice_in_dim(pair_group, own_index * captions, captions)

    unit_image, image_scale = unit_rows(images.astype(jnp.float32))
    image_half = unit_image.astype(jnp.bfloat16)
    image_all = lax.all_gather(image_half, "dp", tiled=True)

    tok_float = tokens.astype(jnp.float32)
    normed = layer_norm(tok_float).astype(jnp.bfloat16)
    pre = jnp.dot(normed, w_up, preferred_element_type=jnp.float32)
    value, slope = gelu_pair(pre)
    position = jnp.arange(seq_len, dtype=jnp.int32)
    valid = (position[None, :] < lengths[:, None]).astype(jnp.float32)
    share = valid / jnp.sum(valid, 1, keepdims=True)
    gmean = jnp.sum(value.reshape(captions, seq_len, hidden) * share[:, :, None], 1)
    tmean = jnp.sum(tok_float.reshape(captions, seq_len, width) * share[:, :, None], 1)
    gbar = gmean.astype(jnp.bfloat16)
    gbar_all = lax.all_gather(gbar, "dp", tiled=True)
    partial_value = lax.dot_general(
        gbar, w_down, (((1,), (1,)), ((), ())), preferred_element_type=jnp.float32
    )
    pooled = tmean + (partial_value + passed_along(partial_value, "mp", 1))
    unit_text, text_scale = unit_rows(pooled)
    text_half = unit_text.astype(jnp.bfloat16)
    text_all = lax.all_gather(text_half, "dp", tiled=True)

    logits, signs, coef = pair_coef(text_half, own_group, image_all, pair_group)
    caption_loss = -jnp.sum(jax.nn.log_sigmoid(signs * logits), 1) / total
    text_back = jnp.dot(coef, image_all, preferred_element_type=jnp.float32)
    _, _, coef_cols = pair_coef(image_half, own_group, text_all, pair_group)
    img_back = jnp.dot(coef_cols, text_all, preferred_element_type=jnp.float32)

    pooled_grad = (
        text_back - unit_text * jnp.sum(unit_text * text_back, 1, keepdims=True)
    ) * text_scale
    image_grad = (
        img_back - unit_image * jnp.sum(unit_image * img_back, 1, keepdims=True)
    ) * image_scale
    pooled_half = pooled_grad.astype(jnp.bfloat16)
    pooled_all = lax.all_gather(pooled_half, "dp", tiled=True)
    rows = width // devices
    pooled_rows = lax.dynamic_slice_in_dim(pooled_all, own_index * rows, rows, axis=1)
    down_grad = lax.dot_general(
        pooled_rows, gbar_all, (((0,), (0,)), ((), ())), preferred_element_type=jnp.float32
    )
    hidden_grad = jnp.dot(pooled_half, w_down, preferred_element_type=jnp.float32)
    pre_grad = (
        share[:, :, None] * hidden_grad[:, None, :] * slope.reshape(captions, seq_len, hidden)
    ).astype(jnp.bfloat16)
    pre_grad = pre_grad.reshape(captions * seq_len, hidden)
    up_term = lax.dot_general(
        normed.reshape(captions * seq_len, devices, rows),
        pre_grad,
        (((0,), (0,)), ((), ())),
        preferred_element_type=jnp.float32,
    )
    up_term = with_layout_constraint(up_term, Layout(major_to_minor=(0, 1, 2)))
    up_grad = lax.psum_scatter(up_term, "dp", scatter_dimension=0, tiled=False)
    return (caption_loss, image_grad, up_grad, down_grad)


def solution(mesh):
    in_specs = (P("dp", None), P("dp"), P("dp", None), P(), P(None, "mp"), P(None, "mp"))
    out_specs = (P("dp"), P("dp", None), P("dp", "mp"), P("dp", "mp"))
    return jax.shard_map(
        on_device, mesh=mesh, in_specs=in_specs, out_specs=out_specs, check_vma=False
    )
```

time: 1350 us -> 751 us (0.56)
  waiting for transfers between devices: 1120 us -> 623 us
  local copies, waits for them, and re-layouts: 79 us -> 43.1 us
  matrix products: 84.2 us -> 49.4 us
    ppermute x191 -> x1, waiting for transfers between devices: 502 us -> 1.59 us  [passed_along(): return lax.ppermute(value, axis, pairs)]
    all_gather x0 -> x4, waiting for transfers between devices: none -> 314 us  [the longest x1 104 us: on_device(): pooled_all = lax.all_gather(pooled_half, 'dp', tiled=True)]
    unnamed x3 -> x6, waiting for transfers between devices: 592 us -> 308 us
    dynamic_slice x64 -> x1, local copies, waits for them, and re-layouts: 49 us -> 0.08 us  [on_device(): lax.dynamic_slice_in_dim(pair_group, own_index * captions, captions)]
    dot_general x194 -> x5, matrix products: 64.2 us -> 30.9 us  [the longest x1 18.6 us: on_device(): lax.dot_general(normed.reshape(captions * seq_len, devices, rows), pre_gr...]
    psum x1 -> x0, waiting for transfers between devices: 29.6 us -> none  [on_device(): pooled = tmean + lax.psum(partial_value, 'mp')]
    dot_general x0 -> x1, local copies, waits for them, and re-layouts: none -> 14.7 us  [on_device(): lax.dot_general(normed.reshape(captions * seq_len, devices, rows), pre_gr...]
  transfers between devices with their start and end apart: 193 -> 6, of which waited for: 67 -> 6; matrix products, arithmetic and copies ran while one was open for 7% -> 14% of each run, Pallas kernels for 0% -> 0%
where the time goes in v1:
time: 751 us; the launch traced here: 750 us
  waiting for transfers between devices  623 us (83%)
  matrix products  49.4 us (7%)
  local copies, waits for them, and re-layouts  43.1 us (6%)
  other arithmetic  16.5 us (2%)
  between operations  13.9 us (2%)
    unnamed x6, waiting for transfers between devices  308 us
    all_gather x1, waiting for transfers between devices, on_device(): pooled_all = lax.all_gather(pooled_half, 'dp', tiled=True)  104 us
    all_gather x1, waiting for transfers between devices, on_device(): gbar_all = lax.all_gather(gbar, 'dp', tiled=True)  103 us
    all_gather x1, waiting for transfers between devices, on_device(): image_all = lax.all_gather(image_half, 'dp', tiled=True)  64.5 us
    all_gather x1, waiting for transfers between devices, on_device(): text_all = lax.all_gather(text_half, 'dp', tiled=True)  42.3 us
    dot_general x1, matrix products, on_device(): lax.dot_general(normed.reshape(captions * seq_len, devices, rows), pre_gr...  18.6 us
  transfers between devices with their start and end apart: 6, of which 6 were waited for; matrix products, arithmetic and copies ran while one was open for 14% of the time, Pallas kernels for 0%

profile of v1, /device:TPU:0, one launch (start us, length us, event | category | flops | bytes accessed | tf_op | source)
XLA Modules:
  0.0 749.9 jit_solution(6134080192428204050)
XLA Ops:
  7.2 0.0 all-gather.5.cloned.1.call-start
  7.2 1.0 fusion.31
  8.3 1.5 fusion.25
  9.7 0.0 all-gather.5.cloned.1.call-update
  9.8 0.0 all-gather.7.cloned.1.call-start
  9.8 2.2 convert_reduce_fusion
  12.0 2.4 multiply_reduce_fusion.1
  14.5 0.6 multiply_convert_fusion
  15.1 11.4 %add_multiply_fusion = (f32[1024,2152]{0,1:T(8,128)}, f32[1024,2152]{0,1:T(8,128)}) fusion(bf16[1024,1152]{1,0:T(8,128)(2,1)S(1)} %multiply_convert_fusion, bf16[1152,2152]{0,1:T(8,128)(2,1)S(1)} %copy-done.8), kind=kOutput, calls=%fused_computation.10 | convolution fusion | flops 5094834176 | bytes 24946688 | tf_op jit(solution)/shard_map/dot_general | solution.py:68
  26.6 9.2 %copy.18 = f32[1024,2152]{1,0:T(8,128)} copy(f32[1024,2152]{0,1:T(8,128)} %get-tuple-element.6) | data formatting | bytes 17629184 | tf_op jit(solution)/shard_map/mul | solution.py:27
  35.8 0.2 convert_reduce_fusion.1
  36.0 0.1 convert_divide_fusion
  36.1 4.7 multiply_reduce_fusion
  40.8 0.0 copy-start.3
  40.8 3.2 fusion.69
  44.1 3.4 collective-permute-start
  47.4 1.0 multiply_reduce_fusion.2
  48.4 1.6 collective-permute-done
  50.0 0.1 multiply_reduce_fusion.4
  50.1 0.7 multiply_convert_fusion.2
  50.8 0.0 all-gather.7.cloned.1.call-update
  50.8 0.0 all-gather.11.cloned.1.call-start
  50.9 0.7 all-gather.11.cloned.1.call-update
  51.6 0.0 all-gather.9.cloned.1.call-start
  51.6 0.1 dynamic_slice.6
  51.7 64.5 %all-gather.5.cloned.1.call-done = bf16[1024,1152]{1,0:T(8,128)(2,1)} async-done(((bf16[16,1152]{1,0:T(8,128)(2,1)}), bf16[1024,1152]{1,0:T(8,128)(2,1)}) %all-gather.5.cloned.1.call-update) | async-done | bytes 2359312 | tf_op jit(solution)/shard_map/all_gather | solution.py:64
  116.2 2.5 fusion.37
  118.8 2.3 multiply_reduce_fusion.3
  121.0 0.7 multiply_convert_fusion.1
  121.7 0.0 all-gather.9.cloned.1.call-update
  121.8 0.2 reduce-scatter.5.cloned.1.call-start
  122.0 2.8 copy.19
  124.8 0.1 div.37
  124.9 2.4 reshape.97
  127.4 3.8 fusion.70
  131.2 4.1 mul.218
  135.3 9.6 %copy.20 = f32[1024,2152]{0,1:T(8,128)} copy(f32[1024,2152]{1,0:T(8,128)} %bitcast.24) | data formatting | bytes 17629184 | tf_op jit(solution)/shard_map/mul | solution.py:106
  144.9 18.6 %fusion.7 = f32[64,18,2152]{2,0,1:T(8,128)} fusion(f32[1024,2152]{0,1:T(8,128)} %get-tuple-element.7, f32[1024,2152]{0,1:T(8,128)} %copy.20, f32[1024]{0:T(1024)S(1)} %div.37, bf16[1024,64,18]{0,2,1:T(8,128)(2,1)S(1)} %copy-done.2), kind=kOutput, calls=%fused_computation.14 | convolution fusion | flops 5121277952 | bytes 29908992 | tf_op jit(solution)/shard_map/dot_general | solution.py:109
  163.5 14.7 %copy.22 = f32[64,18,2152]{2,1,0:T(8,128)} copy(f32[64,18,2152]{2,0,1:T(8,128)} %fusion.7) | data formatting | bytes 19832832 | tf_op jit(solution)/shard_map/dot_general | solution.py:109
  178.2 0.0 reduce-scatter.5.cloned.1.call-update
  178.2 0.5 broadcast_multiply_fusion.1
  178.7 42.3 %all-gather.7.cloned.1.call-done = bf16[1024,1152]{1,0:T(8,128)(2,1)} async-done(((bf16[16,1152]{1,0:T(8,128)(2,1)}), bf16[1024,1152]{1,0:T(8,128)(2,1)}) %all-gather.7.cloned.1.call-update) | async-done | bytes 2359312 | tf_op jit(solution)/shard_map/all_gather | solution.py:83
  221.0 3.5 fusion.28
  224.5 0.7 fusion.30
  225.3 102.5 %all-gather.11.cloned.1.call-done = bf16[1024,2152]{1,0:T(8,128)(2,1)} async-done(((bf16[16,2152]{1,0:T(8,128)(2,1)}), bf16[1024,2152]{1,0:T(8,128)(2,1)}) %all-gather.11.cloned.1.call-update) | async-done | bytes 4407312 | tf_op jit(solution)/shard_map/all_gather | solution.py:76
  327.8 104.3 %all-gather.9.cloned.1.call-done = bf16[1024,1152]{1,0:T(8,128)(2,1)} async-done(((bf16[16,1152]{1,0:T(8,128)(2,1)}), bf16[1024,1152]{1,0:T(8,128)(2,1)}) %all-gather.9.cloned.1.call-update) | async-done | bytes 2359312 | tf_op jit(solution)/shard_map/all_gather | solution.py:98
  432.1 3.9 fusion.21
  436.0 307.4 %reduce-scatter.5.cloned.1.call-done = f32[1,18,2152]{2,1,0:T(8,128)} async-done(((f32[64,18,2152]{2,1,0:T(8,128)}), f32[1,18,2152]{2,1,0:T(8,128)}) %reduce-scatter.5.cloned.1.call-update) | async-done | bytes 154960
  (21 shorter events, 0.1 us)
Async XLA Ops:
  7.2 7.3 copy-start
  7.2 109.0 %all-gather.5.cloned.1.call-start = ((), (), s32[]{:S(2)}) async-start(), calls=%async_computation.1 | async-start | bytes 2396160 | tf_op jit(solution)/shard_map/all_gather | solution.py:64
  9.8 211.2 %all-gather.7.cloned.1.call-start = ((), (), s32[]{:S(2)}) async-start(), calls=%async_computation.2 | async-start | bytes 2396160 | tf_op jit(solution)/shard_map/all_gather | solution.py:83
  9.8 5.3 copy-start.8
  15.1 11.5 %copy-start.1 = (bf16[1024,1152]{1,0:T(8,128)(2,1)}, bf16[1024,1152]{1,0:T(8,128)(2,1)S(1)}, u32[]{:S(2)}) copy-start(bf16[1024,1152]{1,0:T(8,128)(2,1)S(1)} %multiply_convert_fusion) | copy-start | bytes 7077892
  26.6 9.2 %copy-start.7 = (s32[16]{0:T(128)S(1)}, s32[16]{0:T(128)}, u32[]{:S(2)}) copy-start(s32[16]{0:T(128)} %param.7) | copy-start | bytes 196
  40.8 10.1 %copy-start.3 = (bf16[16,2152]{1,0:T(8,128)(2,1)}, bf16[16,2152]{1,0:T(8,128)(2,1)S(1)}, u32[]{:S(2)}) copy-start(bf16[16,2152]{1,0:T(8,128)(2,1)S(1)} %multiply_reduce_fusion) | copy-start | bytes 206596
  40.8 10.8 %copy-start.6 = (s32[1024]{0:T(1024)S(1)}, s32[1024]{0:T(1024)}, u32[]{:S(2)}) copy-start(s32[1024]{0:T(1024)} %param.9) | copy-start | bytes 12292
  44.1 5.9 collective-permute-start
  50.8 277.0 %all-gather.11.cloned.1.call-start = ((), (), s32[]{:S(2)}) async-start(), calls=%async_computation.4 | async-start | bytes 4526080 | tf_op jit(solution)/shard_map/all_gather | solution.py:76
  51.6 380.5 %all-gather.9.cloned.1.call-start = ((), (), s32[]{:S(2)}) async-start(), calls=%async_computation.3 | async-start | bytes 2396160 | tf_op jit(solution)/shard_map/all_gather | solution.py:98
  121.8 5.6 copy-start.5
  121.8 621.6 %reduce-scatter.5.cloned.1.call-start = ((), (), s32[]{:S(2)}) async-start(), calls=%async_computation.5 | async-start | bytes 13578240
  135.3 9.6 %copy-start.2 = (bf16[1024,64,18]{0,2,1:T(8,128)(2,1)S(1)}, bf16[1024,64,18]{0,2,1:T(8,128)(2,1)}, u32[]{:S(2)}) copy-start(bf16[1024,64,18]{0,2,1:T(8,128)(2,1)} %reshape.97) | copy-start | bytes 7077892
  178.2 42.8 %copy-start.4 = (bf16[16,1152]{1,0:T(8,128)(2,1)S(1)}, bf16[16,1152]{1,0:T(8,128)(2,1)}, u32[]{:S(2)}) copy-start(bf16[16,1152]{1,0:T(8,128)(2,1)} %param.8) | copy-start | bytes 110596
Sparse Core Ops, SparseCore 0:
  10.3 105.9 all-gather.4
  118.5 102.4 all-gather.6
  223.3 104.4 all-gather.10
  329.4 102.6 all-gather.8
  434.9 308.4 reduce-scatter.4

commit v2 on v1

--- a/solution.py
+++ b/solution.py
@@ -1,11 +1,11 @@
 import jax
 import jax.numpy as jnp
 from jax import lax
-from jax.experimental.layout import Layout, with_layout_constraint
 from jax.sharding import PartitionSpec as P
 
 LOGIT_SCALE = 117.0
 LOGIT_SHIFT = -12.9
+RS_ORDER = (0, 3, 1, 4, 2, 5)
 
 
 def passed_along(value, axis, steps):
@@ -49,6 +49,23 @@
     return (logits, signs, coef)
 
 
+def reduce_scatter_halving(blocks, axis, order):
+    devices = lax.axis_size(axis)
+    own_index = lax.axis_index(axis)
+    depth = devices.bit_length() - 1
+    left = list(range(depth - 1, -1, -1))
+    state = blocks.reshape((2,) * depth + blocks.shape[1:])
+    for bit in order:
+        place = left.index(bit)
+        own_bit = (own_index >> bit) & 1
+        keep = lax.dynamic_index_in_dim(state, own_bit, axis=place, keepdims=False)
+        send = lax.dynamic_index_in_dim(state, 1 - own_bit, axis=place, keepdims=False)
+        pairs = [(source, source ^ (1 << bit)) for source in range(devices)]
+        state = keep + lax.ppermute(send, axis, pairs)
+        left.remove(bit)
+    return state
+
+
 def on_device(tokens, lengths, images, pair_group, w_up, w_down):
     captions = lengths.shape[0]
     seq_len = tokens.shape[0] // captions
@@ -57,6 +74,7 @@
     devices = lax.axis_size("dp")
     own_index = lax.axis_index("dp")
     total = captions * devices
+    rows = width // devices
     own_group = lax.dynamic_slice_in_dim(pair_group, own_index * captions, captions)
 
     unit_image, image_scale = unit_rows(images.astype(jnp.float32))
@@ -73,20 +91,27 @@
     gmean = jnp.sum(value.reshape(captions, seq_len, hidden) * share[:, :, None], 1)
     tmean = jnp.sum(tok_float.reshape(captions, seq_len, width) * share[:, :, None], 1)
     gbar = gmean.astype(jnp.bfloat16)
-    gbar_all = lax.all_gather(gbar, "dp", tiled=True)
     partial_value = lax.dot_general(
         gbar, w_down, (((1,), (1,)), ((), ())), preferred_element_type=jnp.float32
     )
     pooled = tmean + (partial_value + passed_along(partial_value, "mp", 1))
-    unit_text, text_scale = unit_rows(pooled)
-    text_half = unit_text.astype(jnp.bfloat16)
-    text_all = lax.all_gather(text_half, "dp", tiled=True)
+    gathered = lax.all_gather(
+        jnp.concatenate([pooled, gbar.astype(jnp.float32)], 1), "dp", tiled=True
+    )
+    pooled_all = gathered[:, :width]
+    gbar_all = gathered[:, width:].astype(jnp.bfloat16)
 
-    logits, signs, coef = pair_coef(text_half, own_group, image_all, pair_group)
-    caption_loss = -jnp.sum(jax.nn.log_sigmoid(signs * logits), 1) / total
+    unit_text, text_scale = unit_rows(pooled_all)
+    text_all = unit_text.astype(jnp.bfloat16)
+    logits, signs, coef = pair_coef(text_all, pair_group, image_all, pair_group)
+    own_logits = lax.dynamic_slice_in_dim(logits, own_index * captions, captions)
+    own_signs = lax.dynamic_slice_in_dim(signs, own_index * captions, captions)
+    caption_loss = -jnp.sum(jax.nn.log_sigmoid(own_signs * own_logits), 1) / total
     text_back = jnp.dot(coef, image_all, preferred_element_type=jnp.float32)
-    _, _, coef_cols = pair_coef(image_half, own_group, text_all, pair_group)
-    img_back = jnp.dot(coef_cols, text_all, preferred_element_type=jnp.float32)
+    coef_cols = lax.dynamic_slice_in_dim(coef, own_index * captions, captions, axis=1)
+    img_back = lax.dot_general(
+        coef_cols, text_all, (((0,), (0,)), ((), ())), preferred_element_type=jnp.float32
+    )
 
     pooled_grad = (
         text_back - unit_text * jnp.sum(unit_text * text_back, 1, keepdims=True)
@@ -94,10 +119,9 @@
     image_grad = (
         img_back - unit_image * jnp.sum(unit_image * img_back, 1, keepdims=True)
     ) * image_scale
-    pooled_half = pooled_grad.astype(jnp.bfloat16)
-    pooled_all = lax.all_gather(pooled_half, "dp", tiled=True)
-    rows = width // devices
-    pooled_rows = lax.dynamic_slice_in_dim(pooled_all, own_index * rows, rows, axis=1)
+    pooled_all_half = pooled_grad.astype(jnp.bfloat16)
+    pooled_half = lax.dynamic_slice_in_dim(pooled_all_half, own_index * captions, captions)
+    pooled_rows = lax.dynamic_slice_in_dim(pooled_all_half, own_index * rows, rows, axis=1)
     down_grad = lax.dot_general(
         pooled_rows, gbar_all, (((0,), (0,)), ((), ())), preferred_element_type=jnp.float32
     )
@@ -112,8 +136,7 @@
         (((0,), (0,)), ((), ())),
         preferred_element_type=jnp.float32,
     )
-    up_term = with_layout_constraint(up_term, Layout(major_to_minor=(0, 1, 2)))
-    up_grad = lax.psum_scatter(up_term, "dp", scatter_dimension=0, tiled=False)
+    up_grad = reduce_scatter_halving(up_term, "dp", RS_ORDER)
     return (caption_loss, image_grad, up_grad, down_grad)
 
 

time: 751 us -> 511 us (0.68)
  waiting for transfers between devices: 623 us -> 325 us
  other arithmetic: 16.5 us -> 37.4 us
  matrix products: 49.4 us -> 60.9 us
  local copies, waits for them, and re-layouts: 43.1 us -> 54 us
  starting transfers between devices: 3.74 us -> 11.6 us
    unnamed x6 -> x2, waiting for transfers between devices: 308 us -> 0.03 us
    all_gather x3 -> x1, waiting for transfers between devices: 249 us -> 114 us  [on_device(): lax.all_gather(jnp.concatenate([pooled, gbar.astype(jnp.float32)], 1), 'd...]
    ppermute x0 -> x6, waiting for transfers between devices: none -> 107 us  [reduce_scatter_halving(): state = keep + lax.ppermute(send, axis, pairs)]
    all_gather x1, waiting for transfers between devices: 64.5 us -> 102 us  [on_device(): image_all = lax.all_gather(image_half, 'dp', tiled=True)]
    dynamic_slice x1 -> x7, local copies, waits for them, and re-layouts: 0.08 us -> 23.1 us  [the longest x4 13.5 us: reduce_scatter_halving(): keep = lax.dynamic_index_in_dim(state, own_bit, axis=place, keepdims=False)]
    add x0 -> x7, other arithmetic: none -> 16 us  [the longest x6 16 us: reduce_scatter_halving(): state = keep + lax.ppermute(send, axis, pairs)]
    dot_general x1 -> x0, local copies, waits for them, and re-layouts: 14.7 us -> none  [on_device(): lax.dot_general(normed.reshape(captions * seq_len, devices, rows), pre_gr...]
    ppermute x0 -> x6, starting transfers between devices: none -> 7.96 us  [reduce_scatter_halving(): state = keep + lax.ppermute(send, axis, pairs)]
  transfers between devices with their start and end apart: 6 -> 9, of which waited for: 6 -> 9; matrix products, arithmetic and copies ran while one was open for 14% -> 4% of each run, Pallas kernels for 0% -> 0%
where the time goes in v2:
time: 511 us; the launch traced here: 504 us
  waiting for transfers between devices  325 us (64%)
  matrix products  60.9 us (12%)
  local copies, waits for them, and re-layouts  54 us (11%)
  other arithmetic  37.4 us (7%)
  between operations  14.8 us (3%)
  starting transfers between devices  11.6 us (2%)
    all_gather x1, waiting for transfers between devices, on_device(): lax.all_gather(jnp.concatenate([pooled, gbar.astype(jnp.float32)], 1), 'd...  114 us
    ppermute x6, waiting for transfers between devices, reduce_scatter_halving(): state = keep + lax.ppermute(send, axis, pairs)  107 us
    all_gather x1, waiting for transfers between devices, on_device(): image_all = lax.all_gather(image_half, 'dp', tiled=True)  102 us
    dot_general x1, matrix products, on_device(): lax.dot_general(normed.reshape(captions * seq_len, devices, rows), pre_gr...  16.9 us
    add x6, other arithmetic, reduce_scatter_halving(): state = keep + lax.ppermute(send, axis, pairs)  16 us
    mul x2, local copies, waits for them, and re-layouts, on_device(): share[:, :, None] * hidden_grad[:, None, :]  13.6 us
    dynamic_slice x4, local copies, waits for them, and re-layouts, reduce_scatter_halving(): keep = lax.dynamic_index_in_dim(state, own_bit, axis=place, keepdims=False)  13.5 us
    dot_general x1, matrix products, on_device(): pre = jnp.dot(normed, w_up, preferred_element_type=jnp.float32)  11.5 us
  transfers between devices with their start and end apart: 9, of which 9 were waited for; matrix products, arithmetic and copies ran while one was open for 4% of the time, Pallas kernels for 0%

profile of v2, /device:TPU:0, one launch (start us, length us, event | category | flops | bytes accessed | tf_op | source)
XLA Modules:
  0.0 503.6 jit_solution(1349179237462694615)
XLA Ops:
  7.2 1.0 convert_reduce_fusion.1
  8.2 2.2 convert_reduce_fusion
  10.4 2.4 multiply_reduce_fusion.3
  13.6 11.5 %add_multiply_fusion = (f32[1024,2152]{0,1:T(8,128)}, f32[1024,2152]{0,1:T(8,128)}) fusion(bf16[1024,1152]{1,0:T(8,128)(2,1)S(1)} %multiply_convert_fusion.1, bf16[1152,2152]{0,1:T(8,128)(2,1)S(1)} %copy-done.7), kind=kOutput, calls=%fused_computation.11 | convolution fusion | flops 5094834176 | bytes 24946688 | tf_op jit(solution)/shard_map/dot_general | solution.py:86
  25.2 9.2 %copy.34 = f32[1024,2152]{1,0:T(8,128)} copy(f32[1024,2152]{0,1:T(8,128)} %get-tuple-element.14) | data formatting | bytes 17629184 | tf_op jit(solution)/shard_map/mul | solution.py:27
  34.4 4.7 multiply_reduce_fusion
  39.1 3.2 fusion.42
  42.3 3.4 collective-permute-start
  45.7 1.0 multiply_reduce_fusion.4
  46.7 1.6 collective-permute-done
  48.2 0.7 pad_maximum_fusion
  49.3 0.7 fusion.22
  50.1 2.8 copy.35
  53.0 2.5 reshape.99
  55.5 114.4 %all-gather.3.cloned.1.call-done = f32[1024,3304]{1,0:T(8,128)} async-done(((f32[16,3304]{1,0:T(8,128)}), f32[1024,3304]{1,0:T(8,128)}) %all-gather.3.cloned.1.call-update) | async-done | bytes 13533200 | tf_op jit(solution)/shard_map/all_gather | solution.py:98
  169.9 2.7 multiply_reduce_fusion.2
  172.7 102.0 %all-gather.5.cloned.1.call-done = bf16[1024,1152]{1,0:T(8,128)(2,1)} async-done(((bf16[16,1152]{1,0:T(8,128)(2,1)}), bf16[1024,1152]{1,0:T(8,128)(2,1)}) %all-gather.5.cloned.1.call-update) | async-done | bytes 2359312 | tf_op jit(solution)/shard_map/all_gather | solution.py:82
  274.7 10.5 %multiply_convert_fusion.2 = (bf16[1024,1024]{1,0:T(8,128)(2,1)S(1)}, f32[1024,1024]{1,0:T(8,128)}, f32[1024,1024]{1,0:T(8,128)}) fusion(s32[1024]{0:T(1024)S(1)} %copy-done.9, bf16[1024,1152]{1,0:T(8,128)(2,1)} %all-gather.5.cloned.1.call-done, f32[1024,3304]{1,0:T(8,128)} %all-gather.3.cloned.1.call-done, f32[1024]{0:T(1024)S(1)} %add_rsqrt_fusion), kind=kOutput, calls=%fused_computation.29 | convolution fusion | flops 2430861312 | bytes 17575936 | tf_op jit(solution)/shard_map/dot_general | solution.py:42
  285.2 5.7 %multiply_reduce_fusion.1 = (f32[1024]{0:T(1024)S(1)}, f32[1024,1152]{1,0:T(8,128)S(1)}) fusion(f32[1024,3304]{1,0:T(8,128)} %all-gather.3.cloned.1.call-done, f32[1024]{0:T(1024)S(1)} %add_rsqrt_fusion, bf16[1024,1024]{1,0:T(8,128)(2,1)S(1)} %get-tuple-element.12, bf16[1024,1152]{1,0:T(8,128)(2,1)S(1)} %copy-done.8), kind=kOutput, calls=%fused_computation.15 | convolution fusion | flops 2419457024 | bytes 13901824 | tf_op jit(solution)/shard_map/dot_general | solution.py:110
  290.9 2.9 multiply_convert_fusion
  293.8 4.7 fusion.28
  298.5 4.0 mul.216
  302.5 9.6 %copy.36 = f32[1024,2152]{0,1:T(8,128)} copy(f32[1024,2152]{1,0:T(8,128)} %bitcast.52) | data formatting | bytes 17629184 | tf_op jit(solution)/shard_map/mul | solution.py:130
  312.1 16.9 %fusion.8 = f32[2,2,2,2,2,2,18,2152]{7,6,5,4,3,2,1,0:T(8,128)} fusion(bf16[2,2,2,2,2,2,18,1024]{7,6,5,4,3,2,1,0:T(8,128)(2,1)S(1)} %bitcast.53, f32[1024,2152]{0,1:T(8,128)} %get-tuple-element.15, f32[1024,2152]{0,1:T(8,128)} %copy.36, f32[1024]{0:T(1024)S(1)} %div.34), kind=kOutput, calls=%fused_computation.22 | convolution fusion | flops 5121277952 | bytes 29908992 | tf_op jit(solution)/shard_map/dot_general | solution.py:133
  329.0 10.5 %constant_dynamic-slice_fusion.7 = (f32[2,2,2,2,2,1,18,2152]{7,6,5,4,3,2,1,0:T(8,128)}, f32[2,2,2,2,2,1,18,2152]{7,6,5,4,3,2,1,0:T(8,128)}) fusion(f32[2,2,2,2,2,2,18,2152]{7,6,5,4,3,2,1,0:T(8,128)} %fusion.8, s32[]{:T(128)S(6)} %select_n.63, s32[]{:T(128)S(6)} %select_n.64), kind=kLoop, calls=%fused_computation.75 | loop fusion | bytes 19832840 | tf_op jit(solution)/shard_map/jit(dynamic_index_in_dim)/dynamic_slice | solution.py:61
  339.5 7.7 %copy.54 = f32[2,2,2,2,2,1,18,2152]{7,4,6,3,2,1,0,5:T(2,128)} copy(f32[2,2,2,2,2,1,18,2152]{7,6,5,4,3,2,1,0:T(8,128)} %get-tuple-element.5) | data formatting | bytes 9916416 | tf_op jit(solution)/shard_map/jit(dynamic_index_in_dim)/dynamic_slice | solution.py:62
  347.7 8.4 %collective-permute-done.1 = f32[2,2,2,2,2,18,2152]{6,4,5,3,2,1,0:T(2,128)} collective-permute-done((f32[2,2,2,2,2,18,2152]{6,4,5,3,2,1,0:T(2,128)}, f32[2,2,2,2,2,18,2152]{6,4,5,3,2,1,0:T(2,128)}, u32[]{:S(2)}, u32[]{:S(2)}) %collective-permute-start.1) | collective-permute-done | bytes 4958240 | tf_op jit(solution)/shard_map/ppermute | solution.py:64
  356.1 10.1 %bitcast_add_fusion = f32[2,2,2,2,2,18,2152]{6,4,5,3,2,1,0:T(2,128)} fusion(f32[2,2,2,2,2,18,2152]{6,4,5,3,2,1,0:T(2,128)} %collective-permute-done.1, f32[2,2,2,2,2,1,18,2152]{7,6,5,4,3,2,1,0:T(8,128)} %get-tuple-element.4), kind=kLoop, calls=%fused_computation.12 | loop fusion | flops 1239552 | bytes 14874624 | tf_op jit(solution)/shard_map/add | solution.py:64
  366.2 2.6 dynamic-slice_bitcast_fusion
  368.8 1.0 collective-permute-start.2
  369.8 55.7 %collective-permute-done.2 = f32[2,2,2,2,18,2152]{5,3,4,2,1,0:T(2,128)} collective-permute-done((f32[2,2,2,2,18,2152]{5,3,4,2,1,0:T(2,128)S(1)}, f32[2,2,2,2,18,2152]{5,3,4,2,1,0:T(2,128)}, u32[]{:S(2)}, u32[]{:S(2)}) %collective-permute-start.2) | collective-permute-done | bytes 2479136 | tf_op jit(solution)/shard_map/ppermute | solution.py:64
  425.5 3.8 bitcast_add_fusion.1
  429.3 2.2 constant_dynamic-slice_fusion.5
  431.4 1.7 copy.55
  433.1 0.9 collective-permute-start.3
  434.1 28.1 %collective-permute-done.3 = f32[2,2,2,18,2152]{4,2,3,1,0:T(2,128)S(1)} collective-permute-done((f32[2,2,2,18,2152]{4,2,3,1,0:T(2,128)}, f32[2,2,2,18,2152]{4,2,3,1,0:T(2,128)S(1)}, u32[]{:S(2)}, u32[]{:S(2)}) %collective-permute-start.3) | collective-permute-done | bytes 1239584 | tf_op jit(solution)/shard_map/ppermute | solution.py:64
  462.1 0.9 bitcast_add_fusion.2
  463.1 1.3 collective-permute-start.4
  464.4 3.2 fusion.23
  467.5 1.0 fusion.27
  468.6 0.7 fusion.25
  469.3 8.7 %collective-permute-done.4 = f32[2,2,18,2152]{3,1,2,0:T(2,128)S(1)} collective-permute-done((f32[2,2,18,2152]{3,1,2,0:T(2,128)S(1)}, f32[2,2,18,2152]{3,1,2,0:T(2,128)S(1)}, u32[]{:S(2)}, u32[]{:S(2)}) %collective-permute-start.4) | collective-permute-done | bytes 619808 | tf_op jit(solution)/shard_map/ppermute | solution.py:64
  479.1 2.1 collective-permute-start.5
  481.2 5.2 %fusion.7 = f32[18,2152]{1,0:T(8,128)} fusion(f32[1024,3304]{1,0:T(8,128)} %all-gather.3.cloned.1.call-done, bf16[1024,1152]{1,0:T(8,128)(2,1)} %copy-done.3, s32[]{:T(128)S(6)} %select_n.75), kind=kOutput, calls=%fused_computation.20 | convolution fusion | flops 79331328 | bytes 4873540 | tf_op jit(solution)/shard_map/dot_general | solution.py:125
  486.4 1.2 collective-permute-done.5
  488.1 2.2 collective-permute-start.6
  490.8 4.7 collective-permute-done.6
  495.5 0.7 bitcast_add_fusion.5
  (43 shorter events, 3.8 us)
Async XLA Ops:
  7.2 5.7 %copy-start.6 = (s32[16]{0:T(128)S(1)}, s32[16]{0:T(128)}, u32[]{:S(2)}) copy-start(s32[16]{0:T(128)} %param.7) | copy-start | bytes 196
  7.2 5.8 %copy-start = (bf16[1024,1152]{1,0:T(8,128)(2,1)S(1)}, bf16[1024,1152]{1,0:T(8,128)(2,1)}, u32[]{:S(2)}) copy-start(bf16[1024,1152]{1,0:T(8,128)(2,1)} %param.6) | copy-start | bytes 7077892
  7.2 162.8 %all-gather.3.cloned.1.call-start = ((), (), s32[]{:S(2)}) async-start(), calls=%async_computation | async-start | bytes 13844480 | tf_op jit(solution)/shard_map/all_gather | solution.py:98
  8.2 5.4 %copy-start.7 = (bf16[1152,2152]{0,1:T(8,128)(2,1)S(1)}, bf16[1152,2152]{0,1:T(8,128)(2,1)}, u32[]{:S(2)}) copy-start(bf16[1152,2152]{0,1:T(8,128)(2,1)} %param.10) | copy-start | bytes 14874628
  13.6 11.6 %copy-start.1 = (bf16[1024,1152]{1,0:T(8,128)(2,1)}, bf16[1024,1152]{1,0:T(8,128)(2,1)S(1)}, u32[]{:S(2)}) copy-start(bf16[1024,1152]{1,0:T(8,128)(2,1)S(1)} %multiply_convert_fusion.1) | copy-start | bytes 7077892
  39.1 10.1 %copy-start.4 = (bf16[16,1152]{1,0:T(8,128)(2,1)S(1)}, bf16[16,1152]{1,0:T(8,128)(2,1)}, u32[]{:S(2)}) copy-start(bf16[16,1152]{1,0:T(8,128)(2,1)} %param.8) | copy-start | bytes 110596
  42.3 5.9 %collective-permute-start = (f32[16,1152]{1,0:T(8,128)S(1)}, f32[16,1152]{1,0:T(8,128)S(1)}, u32[]{:S(2)}, u32[]{:S(2)}) collective-permute-start(f32[16,1152]{1,0:T(8,128)S(1)} %fusion.42), channel_id=1, source_target_pairs={{0,1},{1,0},{2,3},{3,2},{4,5},{5,4},{6,7},{7,6},{8,9},{9,8},{10,11... | collective-permute-start | bytes 221192 | tf_op jit(solution)/shard_map/ppermute | solution.py:14
  49.0 225.7 %all-gather.5.cloned.1.call-start = ((), (), s32[]{:S(2)}) async-start(), calls=%async_computation.1 | async-start | bytes 2396160 | tf_op jit(solution)/shard_map/all_gather | solution.py:82
  53.0 221.7 %copy-start.9 = (s32[1024]{0:T(1024)S(1)}, s32[1024]{0:T(1024)}, u32[]{:S(2)}) copy-start(s32[1024]{0:T(1024)} %param.9) | copy-start | bytes 12292
  274.7 10.5 %copy-start.8 = (bf16[1024,1152]{1,0:T(8,128)(2,1)S(1)}, bf16[1024,1152]{1,0:T(8,128)(2,1)}, u32[]{:S(2)}) copy-start(bf16[1024,1152]{1,0:T(8,128)(2,1)} %all-gather.5.cloned.1.call-done) | copy-start | bytes 7077892
  285.2 5.7 %copy-start.5 = (bf16[1024,1024]{1,0:T(8,128)(2,1)}, bf16[1024,1024]{1,0:T(8,128)(2,1)S(1)}, u32[]{:S(2)}) copy-start(bf16[1024,1024]{1,0:T(8,128)(2,1)S(1)} %get-tuple-element.12) | copy-start | bytes 6291460
  293.8 8.7 %copy-start.3 = (bf16[1024,1152]{1,0:T(8,128)(2,1)}, bf16[1024,1152]{1,0:T(8,128)(2,1)S(1)}, u32[]{:S(2)}) copy-start(bf16[1024,1152]{1,0:T(8,128)(2,1)S(1)} %multiply_convert_fusion) | copy-start | bytes 7077892
  302.5 9.6 %copy-start.2 = (bf16[1024,64,18]{0,2,1:T(8,128)(2,1)S(1)}, bf16[1024,64,18]{0,2,1:T(8,128)(2,1)}, u32[]{:S(2)}) copy-start(bf16[1024,64,18]{0,2,1:T(8,128)(2,1)} %reshape.99) | copy-start | bytes 7077892
  347.2 8.9 %collective-permute-start.1 = (f32[2,2,2,2,2,18,2152]{6,4,5,3,2,1,0:T(2,128)}, f32[2,2,2,2,2,18,2152]{6,4,5,3,2,1,0:T(2,128)}, u32[]{:S(2)}, u32[]{:S(2)}) collective-permute-start(f32[2,2,2,2,2,18,2152]{6,4,5,3,2,1,0:T(2,128)} %bitcast.48), channel_id=1, source_target_pairs={{0,2},{2,0},{4,6},{6,4},{8,10},{10,8},{12,14},{14,12},{16,18},{18,... | collective-permute-start | bytes 14874632 | tf_op jit(solution)/shard_map/ppermute | solution.py:64
  368.8 56.7 %collective-permute-start.2 = (f32[2,2,2,2,18,2152]{5,3,4,2,1,0:T(2,128)S(1)}, f32[2,2,2,2,18,2152]{5,3,4,2,1,0:T(2,128)}, u32[]{:S(2)}, u32[]{:S(2)}) collective-permute-start(f32[2,2,2,2,18,2152]{5,3,4,2,1,0:T(2,128)S(1)} %dynamic-slice_bitcast_fusion), channel_id=1, source_target_pairs={{0,16},{2,18},{4,20},{6,22},{8,24},{10,26},{12,28},{14,30},{16,0},... | collective-permute-start | bytes 7437320 | tf_op jit(solution)/shard_map/ppermute | solution.py:64
  433.1 29.0 %collective-permute-start.3 = (f32[2,2,2,18,2152]{4,2,3,1,0:T(2,128)}, f32[2,2,2,18,2152]{4,2,3,1,0:T(2,128)S(1)}, u32[]{:S(2)}, u32[]{:S(2)}) collective-permute-start(f32[2,2,2,18,2152]{4,2,3,1,0:T(2,128)} %bitcast.49), channel_id=1, source_target_pairs={{0,4},{2,6},{4,0},{6,2},{8,12},{10,14},{12,8},{14,10},{16,20},{18,... | collective-permute-start | bytes 3718664 | tf_op jit(solution)/shard_map/ppermute | solution.py:64
  463.1 14.9 %collective-permute-start.4 = (f32[2,2,18,2152]{3,1,2,0:T(2,128)S(1)}, f32[2,2,18,2152]{3,1,2,0:T(2,128)S(1)}, u32[]{:S(2)}, u32[]{:S(2)}) collective-permute-start(f32[2,2,18,2152]{3,1,2,0:T(2,128)S(1)} %dynamic-slice_bitcast_fusion.1), channel_id=1, source_target_pairs={{0,32},{2,34},{4,36},{6,38},{8,40},{10,42},{12,44},{14,46},{16,48}... | collective-permute-start | bytes 1859336 | tf_op jit(solution)/shard_map/ppermute | solution.py:64
  479.1 8.5 %collective-permute-start.5 = (f32[2,18,2152]{2,0,1:T(2,128)S(1)}, f32[2,18,2152]{2,0,1:T(2,128)S(1)}, u32[]{:S(2)}, u32[]{:S(2)}) collective-permute-start(f32[2,18,2152]{2,0,1:T(2,128)S(1)} %bitcast.54), channel_id=1, source_target_pairs={{0,8},{2,10},{4,12},{6,14},{8,0},{10,2},{12,4},{14,6},{16,24},{18,... | collective-permute-start | bytes 929672 | tf_op jit(solution)/shard_map/ppermute | solution.py:64
  488.1 7.4 %collective-permute-start.6 = (f32[18,2152]{1,0:T(8,128)S(1)}, f32[18,2152]{1,0:T(8,128)S(1)}, u32[]{:S(2)}, u32[]{:S(2)}) collective-permute-start(f32[18,2152]{1,0:T(8,128)S(1)} %bitcast.55), channel_id=1, source_target_pairs={{0,64},{2,66},{4,68},{6,70},{8,72},{10,74},{12,76},{14,78},{16,80}... | collective-permute-start | bytes 464840 | tf_op jit(solution)/shard_map/ppermute | solution.py:64
Sparse Core Ops, SparseCore 0:
  49.1 120.7 all-gather.2
  172.2 102.4 all-gather.4
